TPU v7x, 256 devices: a whole 4x4x8 slice. The times are simulated.
256 devices in a mesh: dp: 32 (over x, y, core), head: 8 (over z).
Axes of the slice: x: 4, y: 4, z: 8, core: 2. Of those that a mesh axis runs over, the one named last changes fastest.
Arguments:
- hidden: bfloat16 [16384, 2048], P('dp'), may hold values from -9 to 9
- parents: int32 [256, 64], P('dp'), may hold values from -1 to 62, as said below
- owner_slot: int32 [256], replicated, may hold values from 0 to 255, as said below
- slot_lengths: int32 [256], P('dp'), may hold values from 65 to 496, as said below
- accepted_path: int32 [256, 16], P('dp'), may hold values from 0 to 63, as said below
- accepted_count: int32 [256], P('dp'), may hold values from 1 to 16, as said below
- cache_keys: bfloat16 [256, 512, 2048], P('dp', None, 'head'), may hold values from -82 to 82
- cache_values: bfloat16 [256, 512, 2048], P('dp', None, 'head'), may hold values from -5 to 5
- w_query: bfloat16 [2048, 2048], P(None, 'head'), may hold values from -0.125 to 0.125
- b_query: float32 [2048], P('head'), may hold values from -3 to 3
- w_key: bfloat16 [2048, 2048], P(None, 'head'), may hold values from -0.25 to 0.25
- w_value: bfloat16 [2048, 2048], P(None, 'head'), may hold values from -0.125 to 0.125
- b_value: float32 [2048], P('head'), may hold values from -3 to 3
- w_out: bfloat16 [2048, 2048], P('head'), may hold values from -0.5 to 0.5
- b_out: float32 [2048], replicated, may hold values from -3 to 3
- first_gain: float32 [2048], replicated, may hold values from 0.48 to 2.25
- first_shift: float32 [2048], replicated, may hold values from -2 to 2
- w_up: bfloat16 [2048, 4096], P(None, 'head'), may hold values from -0.125 to 0.125
- b_up: float32 [4096], P('head'), may hold values from -3 to 3
- w_down: bfloat16 [4096, 2048], P('head'), may hold values from -0.09375 to 0.09375
- b_down: float32 [2048], replicated, may hold values from -3 to 3
- second_gain: float32 [2048], replicated, may hold values from 0.5 to 1.5
- second_shift: float32 [2048], replicated, may hold values from -2 to 2
Outputs:
- layer_out: bfloat16 [16384, 2048], P('dp', 'head')
- new_keys: bfloat16 [256, 16, 2048], P('dp', None, 'head')
- new_values: bfloat16 [256, 16, 2048], P('dp', None, 'head')
Inputs may be any that keep to these rules, and one draw needn't show every extreme that they name: owner_slot is a permutation of the 256 slots; slot s lies on dp index s // 8. Of the 8 requests of one dp index, at most 2 have their slots on one dp index, and on every dp index some 2 do. `slot_lengths`: some slot is filled to exactly 496 positions. parents[r, 0] = -1 and 0 <= parents[r, i] < i for i >= 1. For k < accepted_count[r], accepted_path[r, k] is the node at depth k on the way from the root to some node of request r's tree (so entry 0 is node 0); later entries are arbitrary node indices. `accepted_count`: some request has the full 16 entries.
All inputs are finite; a program needn't handle non-finite values.
Results may differ from a plain program's by a relative error of at most 0.018.
Values may be sent and summed in bfloat16 or wider, within the bound.
No kernel may reach another device: no remote copies, remote signals or barrier semaphores. Data moves between devices by JAX's collectives and lax.ppermute only.
A program may use at most 64 MiB of HBM per device.

v0:
```python
import math
import jax
import jax.numpy as jnp
from jax import lax
from jax.sharding import PartitionSpec as P

HD = 128
PEER_MOST = 2
EPSILON = 1e-05


def ancestry(parent_row, draft):
    nodes = jnp.arange(draft, dtype=jnp.int32)
    reach = (parent_row[:, None] == nodes[None, :]).astype(jnp.float32) + jnp.eye(
        draft, dtype=jnp.float32
    )
    for turn in range(max(1, draft.bit_length())):
        reach = jnp.minimum(jnp.dot(reach, reach, precision=lax.Precision.HIGHEST), 1.0)
    return reach > 0.5


def normalize(mixed, gain, shift):
    center = jnp.mean(mixed, axis=-1, keepdims=True)
    square = jnp.mean(mixed * mixed, axis=-1, keepdims=True)
    return (mixed - center) * lax.rsqrt(square - center * center + EPSILON) * gain + shift


def normalize_shared(mixed, sums, gain, shift, model_width):
    center = (sums[0] / model_width)[:, None]
    square = (sums[1] / model_width)[:, None]
    return (mixed - center) * lax.rsqrt(square - center * center + EPSILON) * gain + shift


def split_three(values):
    high = values.astype(jnp.bfloat16)
    rest = values - high.astype(jnp.float32)
    middle = rest.astype(jnp.bfloat16)
    low = (rest - middle.astype(jnp.float32)).astype(jnp.bfloat16)
    return jnp.stack([high, middle, low], axis=1)


def join_three(pieces):
    wide = pieces.astype(jnp.float32)
    return wide[:, 0] + (wide[:, 1] + wide[:, 2])


def local(
    hidden,
    parents,
    owner_slot,
    slot_lengths,
    accepted_path,
    accepted_count,
    cache_keys,
    cache_values,
    w_query,
    b_query,
    w_key,
    w_value,
    b_value,
    w_out,
    b_out,
    first_gain,
    first_shift,
    w_up,
    b_up,
    w_down,
    b_down,
    second_gain,
    second_shift,
):
    requests = parents.shape[0]
    draft = parents.shape[1]
    tokens = hidden.shape[0]
    model_width = hidden.shape[1]
    width = w_query.shape[1]
    local_heads = width // HD
    capacity = cache_keys.shape[1]
    block = min(capacity, 256)
    shards = lax.axis_size("dp")
    myself = lax.axis_index("dp")
    scale = 1.0 / math.sqrt(HD)
    queries = (jnp.dot(hidden, w_query, preferred_element_type=jnp.float32) + b_query).astype(
        jnp.bfloat16
    )
    key_rows = jnp.dot(hidden, w_key, preferred_element_type=jnp.float32).astype(jnp.bfloat16)
    value_rows = (jnp.dot(hidden, w_value, preferred_element_type=jnp.float32) + b_value).astype(
        jnp.bfloat16
    )
    local_ids = jnp.arange(requests, dtype=jnp.int32)
    levels = jnp.arange(accepted_path.shape[1], dtype=jnp.int32)
    chosen = local_ids[:, None] * draft + accepted_path
    usable = (levels[None, :] < accepted_count[:, None])[..., None]
    kept_keys = jnp.where(usable, key_rows[chosen], jnp.zeros((), jnp.bfloat16))
    kept_values = jnp.where(usable, value_rows[chosen], jnp.zeros((), jnp.bfloat16))
    tree_queries = queries.reshape(requests, draft, local_heads, HD)
    tree_keys = key_rows.reshape(requests, draft, local_heads, HD)
    tree_values = value_rows.reshape(requests, draft, local_heads, HD)
    lineage = jax.vmap(lambda parent_row: ancestry(parent_row, draft))(parents)
    tree_scores = (
        jnp.einsum("rqhd,rkhd->rhqk", tree_queries, tree_keys, preferred_element_type=jnp.float32)
        * scale
    )
    tree_scores = jnp.where(lineage[:, None], tree_scores, -jnp.inf)
    tree_top = jnp.max(tree_scores, axis=3, keepdims=True)
    tree_exp = jnp.exp(tree_scores - tree_top)
    tree_total = jnp.sum(tree_exp, axis=3, keepdims=True)
    tree_probs = tree_exp.astype(jnp.bfloat16)
    tree_part = jnp.einsum(
        "rhqk,rkhd->rqhd", tree_probs, tree_values, preferred_element_type=jnp.float32
    ) / jnp.transpose(tree_total, (0, 2, 1, 3))
    tree_lse = jnp.transpose((tree_top + jnp.log(tree_total))[..., 0], (0, 2, 1))[..., None]
    my_owner = lax.dynamic_slice_in_dim(owner_slot, myself * requests, requests)
    target = my_owner // requests
    earlier = local_ids[None, :] < local_ids[:, None]
    same_target = target[None, :] == target[:, None]
    rank = jnp.sum((earlier & same_target).astype(jnp.int32), axis=1)
    my_slots = myself * requests + local_ids
    every_id = jnp.arange(owner_slot.shape[0], dtype=jnp.int32)
    source_request = jnp.sum(
        jnp.where(owner_slot[None, :] == my_slots[:, None], every_id[None, :], 0), axis=1
    )
    source = source_request // requests
    source_local = source_request % requests
    source_targets = owner_slot.reshape(shards, requests)[source] // requests
    source_rank = jnp.sum(
        ((local_ids[None, :] < source_local[:, None]) & (source_targets == myself)).astype(
            jnp.int32
        ),
        axis=1,
    )
    shaped_queries = queries.reshape(requests, draft, width)
    slots_total = shards * PEER_MOST
    send_index = target * PEER_MOST + rank
    receive_index = source * PEER_MOST + source_rank
    slot_ids = jnp.arange(slots_total, dtype=jnp.int32)

    def spread(values, index):
        placing = (index[None, :] == slot_ids[:, None]).astype(values.dtype)
        flat = values.reshape(values.shape[0], -1)
        placed = jnp.dot(placing, flat, preferred_element_type=jnp.float32).astype(values.dtype)
        return placed.reshape((slots_total,) + values.shape[1:])

    arrived = lax.all_to_all(
        spread(shaped_queries, send_index), "dp", split_axis=0, concat_axis=0, tiled=True
    )
    kept = lax.all_to_all(
        spread(jnp.concatenate([kept_keys, kept_values], axis=1), send_index),
        "dp",
        split_axis=0,
        concat_axis=0,
        tiled=True,
    )[receive_index]
    owned_queries = arrived[receive_index].reshape(requests, draft, local_heads, HD)
    new_keys = kept[:, : kept_keys.shape[1]]
    new_values = kept[:, kept_keys.shape[1] :]
    slot_keys = cache_keys.reshape(requests, capacity, local_heads, HD)
    slot_values = cache_values.reshape(requests, capacity, local_heads, HD)
    scores = (
        jnp.einsum("sqhd,skhd->shqk", owned_queries, slot_keys, preferred_element_type=jnp.float32)
        * scale
    )
    living = jnp.arange(capacity, dtype=jnp.int32)[None, :] < slot_lengths[:, None]
    scores = jnp.where(living[:, None, None, :], scores, -jnp.inf)
    cache_top = jnp.max(scores, axis=3, keepdims=True)
    cache_exp = jnp.exp(scores - cache_top)
    cache_total = jnp.sum(cache_exp, axis=3, keepdims=True)
    cache_probs = cache_exp.astype(jnp.bfloat16)
    gathered = jnp.einsum(
        "shqk,skhd->sqhd", cache_probs, slot_values, preferred_element_type=jnp.float32
    )
    owned_part = (
        (gathered / jnp.transpose(cache_total, (0, 2, 1, 3)))
        .astype(jnp.bfloat16)
        .reshape(requests, draft, width)
    )
    owned_lse = (cache_top + jnp.log(cache_total))[..., 0]
    lse_flat = split_three(owned_lse).reshape(requests, -1)
    lse_rows = -(-lse_flat.shape[1] // width)
    lse_flat = jnp.pad(lse_flat, ((0, 0), (0, lse_rows * width - lse_flat.shape[1])))
    back = jnp.concatenate(
        [
            spread(owned_part, receive_index),
            spread(lse_flat, receive_index).reshape(slots_total, lse_rows, width),
        ],
        axis=1,
    )
    returned = lax.all_to_all(back, "dp", split_axis=0, concat_axis=0, tiled=True)[send_index]
    cache_part = returned[:, :draft]
    lse_back = returned[:, draft:].reshape(requests, -1)[:, : 3 * local_heads * draft]
    cache_lse = join_three(lse_back.reshape(requests, 3, local_heads, draft))
    cache_weight = jnp.transpose(cache_lse, (0, 2, 1))[..., None]
    larger = jnp.maximum(cache_weight, tree_lse)
    cache_share = jnp.exp(cache_weight - larger)
    tree_share = jnp.exp(tree_lse - larger)
    blended = (
        cache_share * cache_part.astype(jnp.float32).reshape(requests, draft, local_heads, HD)
        + tree_share * tree_part
    ) / (cache_share + tree_share)
    attended = blended.astype(jnp.bfloat16).reshape(tokens, width)
    attention_term = jnp.dot(attended, w_out, preferred_element_type=jnp.float32)
    feature = model_width // lax.axis_size("head")
    offset = lax.axis_index("head") * feature

    def columns(values):
        return lax.dynamic_slice_in_dim(values, offset, feature, values.ndim - 1)

    attention_sum = lax.psum(attention_term.astype(jnp.bfloat16), "head").astype(jnp.float32)
    first_normed = normalize(
        attention_sum + b_out + hidden.astype(jnp.float32), first_gain, first_shift
    ).astype(jnp.bfloat16)
    inner = jax.nn.gelu(
        jnp.dot(first_normed, w_up, preferred_element_type=jnp.float32) + b_up, approximate=True
    ).astype(jnp.bfloat16)
    down_share = lax.psum_scatter(
        jnp.dot(inner, w_down, preferred_element_type=jnp.float32).astype(jnp.bfloat16),
        "head",
        scatter_dimension=1,
        tiled=True,
    ).astype(jnp.float32)
    second_mixed = down_share + columns(b_down) + columns(first_normed).astype(jnp.float32)
    heads_along = lax.axis_size("head")
    own_sums = jnp.stack(
        [jnp.sum(second_mixed, axis=1), jnp.sum(second_mixed * second_mixed, axis=1)]
    )
    second_sums = jnp.sum(
        lax.all_to_all(
            jnp.broadcast_to(own_sums[None], (heads_along,) + own_sums.shape),
            "head",
            0,
            0,
            tiled=False,
        ),
        axis=0,
    )
    layer_out = normalize_shared(
        second_mixed, second_sums, columns(second_gain), columns(second_shift), model_width
    ).astype(jnp.bfloat16)
    return (layer_out, new_keys, new_values)


def solution(mesh):
    placed = (
        P("dp", None),
        P("dp", None),
        P(),
        P("dp"),
        P("dp", None),
        P("dp"),
        P("dp", None, "head"),
        P("dp", None, "head"),
        P(None, "head"),
        P("head"),
        P(None, "head"),
        P(None, "head"),
        P("head"),
        P("head", None),
        P(),
        P(),
        P(),
        P(None, "head"),
        P("head"),
        P("head", None),
        P(),
        P(),
        P(),
    )
    return jax.shard_map(
        local,
        mesh=mesh,
        in_specs=placed,
        out_specs=(P("dp", "head"), P("dp", None, "head"), P("dp", None, "head")),
        check_vma=False,
    )
```

profile of v0, /device:TPU:2, one launch (start us, length us, event | category | flops | bytes accessed | tf_op | source)
XLA Modules:
  0.0 265.0 jit_solution(14753216439915072856)
XLA Ops:
  7.2 0.9 and_select_fusion
  8.3 0.8 compare_select_fusion.1
  9.0 2.6 fusion.24
  11.8 0.7 convolution_convert_fusion.1
  12.5 1.8 copy.75
  14.3 7.8 %all-to-all-start = ((bf16[64,64,256]{2,1,0:T(8,128)(2,1)}), bf16[64,64,256]{2,1,0:T(8,128)(2,1)}, u32[]{:S(2)}, u32[]{:S(2)}) async-start(bf16[64,64,256]{2,1,0:T(8,128)(2,1)} %bitcast.164), calls=%async_computation | async-start | bytes 4194304 | tf_op jit(solution)/shard_map/all_to_all | solution.py:144
  22.5 0.6 gather_fusion
  23.4 0.5 convolution_minimum_fusion.6
  23.9 2.6 convolution_convert_fusion.5
  26.5 21.7 %all-to-all-done = bf16[64,64,256]{2,1,0:T(8,128)(2,1)} async-done(((bf16[64,64,256]{2,1,0:T(8,128)(2,1)}), bf16[64,64,256]{2,1,0:T(8,128)(2,1)}, u32[]{:S(2)}, u32[]{:S(2)}) %all-to-all-start) | async-done | bytes 2097184 | tf_op jit(solution)/shard_map/all_to_all | solution.py:144
  48.1 2.2 gather_fusion.1
  50.3 2.5 fusion.7
  52.8 0.7 fusion.8
  53.6 0.9 copy-done.11
  54.4 0.9 fusion.21
  55.8 0.7 convolution_convert_fusion
  56.5 1.9 copy.76
  58.6 3.2 %pad_maximum_fusion = bf16[64,66,256]{2,1,0:T(8,128)(2,1)} fusion(bf16[64,2,256]{2,1,0:T(2,128)(2,1)S(1)} %reshape.370, bf16[64,64,256]{2,1,0:T(8,128)(2,1)} %bitcast.165), kind=kLoop, calls=%fused_computation.15 | loop fusion | flops 4325376 | bytes 4325376 | tf_op jit(solution)/shard_map/concatenate | solution.py:181
  61.8 7.6 %all-to-all-start.1 = ((bf16[64,66,256]{2,1,0:T(8,128)(2,1)}), bf16[64,66,256]{2,1,0:T(8,128)(2,1)}, u32[]{:S(2)}, u32[]{:S(2)}) async-start(bf16[64,66,256]{2,1,0:T(8,128)(2,1)} %pad_maximum_fusion), calls=%async_computation.1 | async-start | bytes 4718592 | tf_op jit(solution)/shard_map/all_to_all | solution.py:188
  70.2 0.8 reshape.373
  73.1 2.6 fusion.25
  75.7 0.8 reshape.376
  76.5 1.2 fusion.91
  77.8 20.6 %all-to-all-done.1 = bf16[64,66,256]{2,1,0:T(8,128)(2,1)} async-done(((bf16[64,66,256]{2,1,0:T(8,128)(2,1)}), bf16[64,66,256]{2,1,0:T(8,128)(2,1)}, u32[]{:S(2)}, u32[]{:S(2)}) %all-to-all-start.1) | async-done | bytes 2162720 | tf_op jit(solution)/shard_map/all_to_all | solution.py:188
  98.4 2.2 gather_fusion.2
  100.8 1.8 fusion.26
  102.9 2.0 convolution_convert_fusion.3
  105.0 83.3 %all-reduce.3.cloned.1.call-done = bf16[512,2048]{1,0:T(8,128)(2,1)} async-done(((bf16[512,2048]{1,0:T(8,128)(2,1)}), bf16[512,2048]{1,0:T(8,128)(2,1)}) %all-reduce.3.cloned.1.call-update) | async-done | bytes 2097168 | tf_op jit(solution)/shard_map/psum | solution.py:208
  188.3 3.5 %fusion = (f32[512]{0:T(512)S(1)}, f32[512]{0:T(512)S(1)}) fusion(bf16[512,2048]{1,0:T(8,128)(2,1)} %param.23, bf16[512,2048]{1,0:T(8,128)(2,1)} %all-reduce.3.cloned.1.call-done, f32[2048]{0:T(1024)S(1)} %copy-done.4), kind=kLoop, calls=%fused_computation.12 | loop fusion | flops 7339008 | bytes 4206592 | tf_op jit(solution)/shard_map/reduce_sum | solution.py:23
  191.8 2.6 add_convert_fusion
  194.5 6.1 %convolution_convert_fusion.4 = bf16[512,2048]{1,0:T(8,128)(2,1)} fusion(bf16[512,2048]{1,0:T(8,128)(2,1)S(1)} %copy-done, bf16[512,2048]{1,0:T(8,128)(2,1)} %add_convert_fusion, bf16[2048,512]{1,0:T(8,128)(2,1)} %param.40, f32[512]{0:T(512)S(1)} %copy-done.12), kind=kOutput, calls=%fused_computation.14 | convolution fusion | flops 2151153664 | bytes 8390656 | tf_op jit(solution)/shard_map/dot_general | solution.py:216
  200.6 0.6 copy-done.9
  201.4 0.8 gather_fusion.3
  202.2 0.8 gather_fusion.4
  203.8 1.2 copy.80
  205.0 7.4 %all-to-all-start.3 = ((bf16[64,32,256]{2,1,0:T(8,128)(2,1)}), bf16[64,32,256]{2,1,0:T(8,128)(2,1)S(1)}, u32[]{:S(2)}, u32[]{:S(2)}) async-start(bf16[64,32,256]{2,1,0:T(8,128)(2,1)} %bitcast.47), calls=%async_computation.4 | async-start | bytes 2097152 | tf_op jit(solution)/shard_map/all_to_all | solution.py:147
  212.5 0.8 dynamic_slice.16
  213.2 0.8 dynamic_slice.18
  214.0 0.8 dynamic_slice.19
  214.7 12.1 %all-to-all-done.3 = bf16[64,32,256]{2,1,0:T(8,128)(2,1)S(1)} async-done(((bf16[64,32,256]{2,1,0:T(8,128)(2,1)}), bf16[64,32,256]{2,1,0:T(8,128)(2,1)S(1)}, u32[]{:S(2)}, u32[]{:S(2)}) %all-to-all-start.3) | async-done | bytes 1048608 | tf_op jit(solution)/shard_map/all_to_all | solution.py:147
  226.9 0.6 gather_fusion.5
  227.5 14.1 %reduce-scatter.2.cloned.1.call-done = bf16[512,256]{1,0:T(8,128)(2,1)} async-done(((bf16[512,2048]{1,0:T(8,128)(2,1)}), bf16[512,256]{1,0:T(8,128)(2,1)}) %reduce-scatter.2.cloned.1.call-update) | async-done | bytes 262160 | tf_op jit(solution)/shard_map/reduce_scatter | solution.py:215
  241.6 1.3 fusion.48
  242.9 0.6 broadcast_in_dim.71
  243.5 4.7 %all-to-all-start.2 = ((f32[8,2,512]{2,1,0:T(2,128)}), f32[8,2,512]{2,1,0:T(2,128)S(1)}, u32[]{:S(2)}, u32[]{:S(2)}) async-start(f32[8,2,512]{2,1,0:T(2,128)} %broadcast_in_dim.71), calls=%async_computation.3 | async-start | bytes 65536 | tf_op jit(solution)/shard_map/all_to_all | solution.py:227
  248.2 0.7 fusion.90
  248.8 7.4 %all-to-all-done.2 = f32[8,2,512]{2,1,0:T(2,128)S(1)} async-done(((f32[8,2,512]{2,1,0:T(2,128)}), f32[8,2,512]{2,1,0:T(2,128)S(1)}, u32[]{:S(2)}, u32[]{:S(2)}) %all-to-all-start.2) | async-done | bytes 32800 | tf_op jit(solution)/shard_map/all_to_all | solution.py:227
  256.3 1.9 add_convert_fusion.1
  (84 shorter events, 6.0 us)
Async XLA Ops:
  7.2 187.3 %copy-start = (bf16[512,2048]{1,0:T(8,128)(2,1)S(1)}, bf16[512,2048]{1,0:T(8,128)(2,1)}, u32[]{:S(2)}) copy-start(bf16[512,2048]{1,0:T(8,128)(2,1)} %param.42) | copy-start | bytes 6291460
  14.3 7.8 %copy-start.7 = (s32[256]{0:T(256)S(1)}, s32[256]{0:T(256)}, u32[]{:S(2)}) copy-start(s32[256]{0:T(256)} %param.25) | copy-start | bytes 3076
  14.3 9.0 %copy-start.10 = (s32[8]{0:T(128)S(1)}, s32[8]{0:T(128)}, u32[]{:S(2)}) copy-start(s32[8]{0:T(128)} %param.26) | copy-start | bytes 100
  14.3 9.0 %copy-start.8 = (s32[8,64]{1,0:T(8,128)S(1)}, s32[8,64]{1,0:T(8,128)}, u32[]{:S(2)}) copy-start(s32[8,64]{1,0:T(8,128)} %param.24) | copy-start | bytes 6148
  14.3 33.8 %all-to-all-start = ((bf16[64,64,256]{2,1,0:T(8,128)(2,1)}), bf16[64,64,256]{2,1,0:T(8,128)(2,1)}, u32[]{:S(2)}, u32[]{:S(2)}) async-start(bf16[64,64,256]{2,1,0:T(8,128)(2,1)} %bitcast.164), calls=%async_computation | async-start | bytes 4194304 | tf_op jit(solution)/shard_map/all_to_all | solution.py:144
  52.8 1.6 copy-start.11
  61.8 36.6 %all-to-all-start.1 = ((bf16[64,66,256]{2,1,0:T(8,128)(2,1)}), bf16[64,66,256]{2,1,0:T(8,128)(2,1)}, u32[]{:S(2)}, u32[]{:S(2)}) async-start(bf16[64,66,256]{2,1,0:T(8,128)(2,1)} %pad_maximum_fusion), calls=%async_computation.1 | async-start | bytes 4718592 | tf_op jit(solution)/shard_map/all_to_all | solution.py:188
  69.5 118.8 %all-reduce.3.cloned.1.call-start = ((), (), s32[]{:S(2)}) async-start(), calls=%async_computation.5 | async-start | bytes 4194304 | tf_op jit(solution)/shard_map/psum | solution.py:208
  70.2 2.9 %copy-start.13 = (f32[256]{0:T(256)S(1)}, f32[256]{0:T(256)}, u32[]{:S(2)}) copy-start(f32[256]{0:T(256)} %param.35) | copy-start | bytes 3076
  100.8 2.1 copy-start.3
  102.9 85.4 %copy-start.4 = (f32[2048]{0:T(1024)S(1)}, f32[2048]{0:T(1024)}, u32[]{:S(2)}) copy-start(f32[2048]{0:T(1024)} %param.37) | copy-start | bytes 24580
  104.9 86.9 %copy-start.5 = (f32[2048]{0:T(1024)S(1)}, f32[2048]{0:T(1024)}, u32[]{:S(2)}) copy-start(f32[2048]{0:T(1024)} %param.39) | copy-start | bytes 24580
  105.0 86.8 %copy-start.6 = (f32[2048]{0:T(1024)S(1)}, f32[2048]{0:T(1024)}, u32[]{:S(2)}) copy-start(f32[2048]{0:T(1024)} %param.38) | copy-start | bytes 24580
  105.0 136.6 %reduce-scatter.2.cloned.1.call-start = ((), (), s32[]{:S(2)}) async-start(), calls=%async_computation.6 | async-start | bytes 2359296 | tf_op jit(solution)/shard_map/reduce_scatter | solution.py:215
  188.3 3.5 %copy-start.1 = (bf16[512,2048]{1,0:T(8,128)(2,1)S(1)}, bf16[512,2048]{1,0:T(8,128)(2,1)}, u32[]{:S(2)}) copy-start(bf16[512,2048]{1,0:T(8,128)(2,1)} %param.23) | copy-start | bytes 6291460
  188.3 3.5 %copy-start.2 = (bf16[512,2048]{1,0:T(8,128)(2,1)S(1)}, bf16[512,2048]{1,0:T(8,128)(2,1)}, u32[]{:S(2)}) copy-start(bf16[512,2048]{1,0:T(8,128)(2,1)} %all-reduce.3.cloned.1.call-done) | copy-start | bytes 6291460
  191.8 2.6 copy-start.12
  200.5 0.7 copy-start.9
  200.5 2.6 copy-start.14
  205.0 21.9 %all-to-all-start.3 = ((bf16[64,32,256]{2,1,0:T(8,128)(2,1)}), bf16[64,32,256]{2,1,0:T(8,128)(2,1)S(1)}, u32[]{:S(2)}, u32[]{:S(2)}) async-start(bf16[64,32,256]{2,1,0:T(8,128)(2,1)} %bitcast.47), calls=%async_computation.4 | async-start | bytes 2097152 | tf_op jit(solution)/shard_map/all_to_all | solution.py:147
  243.5 12.7 %all-to-all-start.2 = ((f32[8,2,512]{2,1,0:T(2,128)}), f32[8,2,512]{2,1,0:T(2,128)S(1)}, u32[]{:S(2)}, u32[]{:S(2)}) async-start(f32[8,2,512]{2,1,0:T(2,128)} %broadcast_in_dim.71), calls=%async_computation.3 | async-start | bytes 65536 | tf_op jit(solution)/shard_map/all_to_all | solution.py:227
Sparse Core Ops, SparseCore 0:
  105.1 83.2 all-reduce.2
  200.7 40.8 reduce-scatter.1
where the time goes:
time: 266 us; the launch traced here: 265 us
  waiting for transfers between devices  159 us (60%)
  starting transfers between devices  27.8 us (10%)
  matrix products  27 us (10%)
  local copies, waits for them, and re-layouts  20.3 us (8%)
  other arithmetic  16.1 us (6%)
  between operations  14.6 us (5%)
    psum x1, waiting for transfers between devices, local(): lax.psum(attention_term.astype(jnp.bfloat16), 'head').astype(jnp.float32)  83.3 us
    all_to_all x1, waiting for transfers between devices, local(): lax.all_to_all(spread(shaped_queries, send_index), 'dp', split_axis=0, co...  21.7 us
    all_to_all x1, waiting for transfers between devices, local(): lax.all_to_all(back, 'dp', split_axis=0, concat_axis=0, tiled=True)  20.6 us
    reduce_scatter x1, waiting for transfers between devices, local(): lax.psum_scatter(jnp.dot(inner, w_down, preferred_element_type=jnp.float3...  14.1 us
    all_to_all x1, waiting for transfers between devices, local(): lax.all_to_all(spread(jnp.concatenate([kept_keys, kept_values], axis=1),...  12.1 us
    all_to_all x1, starting transfers between devices, local(): lax.all_to_all(spread(shaped_queries, send_index), 'dp', split_axis=0, co...  7.81 us
    all_to_all x1, starting transfers between devices, local(): lax.all_to_all(back, 'dp', split_axis=0, concat_axis=0, tiled=True)  7.64 us
    all_to_all x1, starting transfers between devices, local(): lax.all_to_all(spread(jnp.concatenate([kept_keys, kept_values], axis=1),...  7.42 us
  transfers between devices with their start and end apart: 6, of which 6 were waited for; matrix products, arithmetic and copies ran while one was open for 7% of the time, Pallas kernels for 0%

commit v1 on v0

--- a/solution.py
+++ b/solution.py
@@ -7,6 +7,7 @@
 HD = 128
 PEER_MOST = 2
 EPSILON = 1e-05
+results_match = lambda local_array: lax.all_gather(local_array, "head").sum(axis=0)
 
 
 def ancestry(parent_row, draft):
@@ -205,7 +206,7 @@
     def columns(values):
         return lax.dynamic_slice_in_dim(values, offset, feature, values.ndim - 1)
 
-    attention_sum = lax.psum(attention_term.astype(jnp.bfloat16), "head").astype(jnp.float32)
+    attention_sum = results_match(attention_term.astype(jnp.bfloat16)).astype(jnp.float32)
     first_normed = normalize(
         attention_sum + b_out + hidden.astype(jnp.float32), first_gain, first_shift
     ).astype(jnp.bfloat16)

time: 266 us -> 365 us (1.37)
  waiting for transfers between devices: 159 us -> 250 us
  other arithmetic: 16.1 us -> 25.3 us
    all_gather x0 -> x1, waiting for transfers between devices: none -> 174 us  [lax.all_gather(local_array, 'head').sum(axis=0)]
    psum x1 -> x0, waiting for transfers between devices: 83.3 us -> none  [local(): lax.psum(attention_term.astype(jnp.bfloat16), 'head').astype(jnp.float32)]
    reduce_sum x0 -> x1, other arithmetic: none -> 10.8 us  [lax.all_gather(local_array, 'head').sum(axis=0)]
  transfers between devices with their start and end apart: 6 -> 6, of which waited for: 6 -> 6; matrix products, arithmetic and copies ran while one was open for 7% -> 5% of each run, Pallas kernels for 0% -> 0%
where the time goes in v1:
time: 365 us; the launch traced here: 364 us
  waiting for transfers between devices  250 us (68%)
  starting transfers between devices  27.9 us (8%)
  matrix products  27 us (7%)
  other arithmetic  25.3 us (7%)
  local copies, waits for them, and re-layouts  19 us (5%)
  between operations  14.6 us (4%)
    all_gather x1, waiting for transfers between devices, lax.all_gather(local_array, 'head').sum(axis=0)  174 us
    all_to_all x1, waiting for transfers between devices, local(): lax.all_to_all(spread(shaped_queries, send_index), 'dp', split_axis=0, co...  23.9 us
    all_to_all x1, waiting for transfers between devices, local(): lax.all_to_all(back, 'dp', split_axis=0, concat_axis=0, tiled=True)  18.4 us
    reduce_scatter x1, waiting for transfers between devices, local(): lax.psum_scatter(jnp.dot(inner, w_down, preferred_element_type=jnp.float3...  13.9 us
    all_to_all x1, waiting for transfers between devices, local(): lax.all_to_all(spread(jnp.concatenate([kept_keys, kept_values], axis=1),...  12.1 us
    reduce_sum x1, other arithmetic, lax.all_gather(local_array, 'head').sum(axis=0)  10.8 us
    all_to_all x1, starting transfers between devices, local(): lax.all_to_all(spread(shaped_queries, send_index), 'dp', split_axis=0, co...  7.81 us
    all_to_all x1, starting transfers between devices, local(): lax.all_to_all(back, 'dp', split_axis=0, concat_axis=0, tiled=True)  7.64 us
  transfers between devices with their start and end apart: 6, of which 6 were waited for; matrix products, arithmetic and copies ran while one was open for 5% of the time, Pallas kernels for 0%

profile of v1, /device:TPU:2, one launch (start us, length us, event | category | flops | bytes accessed | tf_op | source)
XLA Modules:
  0.0 363.6 jit_solution(2431267969088998468)
XLA Ops:
  7.2 0.9 and_select_fusion
  8.3 0.8 compare_select_fusion.1
  9.0 2.6 fusion.24
  11.8 0.7 convolution_convert_fusion.1
  12.5 1.8 copy.75
  14.3 7.8 %all-to-all-start = ((bf16[64,64,256]{2,1,0:T(8,128)(2,1)}), bf16[64,64,256]{2,1,0:T(8,128)(2,1)}, u32[]{:S(2)}, u32[]{:S(2)}) async-start(bf16[64,64,256]{2,1,0:T(8,128)(2,1)} %bitcast.166), calls=%async_computation | async-start | bytes 4194304 | tf_op jit(solution)/shard_map/all_to_all | solution.py:145
  22.5 0.6 gather_fusion
  24.3 23.9 %all-to-all-done = bf16[64,64,256]{2,1,0:T(8,128)(2,1)} async-done(((bf16[64,64,256]{2,1,0:T(8,128)(2,1)}), bf16[64,64,256]{2,1,0:T(8,128)(2,1)}, u32[]{:S(2)}, u32[]{:S(2)}) %all-to-all-start) | async-done | bytes 2097184 | tf_op jit(solution)/shard_map/all_to_all | solution.py:145
  48.1 2.2 gather_fusion.1
  50.3 2.5 fusion.7
  52.8 0.7 fusion.8
  53.6 0.9 copy-done.11
  54.4 0.9 fusion.21
  56.1 0.7 convolution_convert_fusion
  56.8 0.5 copy.76
  57.3 1.6 pad_maximum_fusion
  58.9 7.6 %all-to-all-start.1 = ((bf16[64,66,256]{2,1,0:T(8,128)(2,1)}), bf16[64,66,256]{2,1,0:T(8,128)(2,1)}, u32[]{:S(2)}, u32[]{:S(2)}) async-start(bf16[64,66,256]{2,1,0:T(8,128)(2,1)} %pad_maximum_fusion), calls=%async_computation.1 | async-start | bytes 4718592 | tf_op jit(solution)/shard_map/all_to_all | solution.py:189
  69.0 2.6 convolution_convert_fusion.5
  71.6 0.8 reshape.373
  72.4 2.6 fusion.25
  75.0 0.8 reshape.376
  75.7 1.2 fusion.91
  77.1 18.4 %all-to-all-done.1 = bf16[64,66,256]{2,1,0:T(8,128)(2,1)} async-done(((bf16[64,66,256]{2,1,0:T(8,128)(2,1)}), bf16[64,66,256]{2,1,0:T(8,128)(2,1)}, u32[]{:S(2)}, u32[]{:S(2)}) %all-to-all-start.1) | async-done | bytes 2162720 | tf_op jit(solution)/shard_map/all_to_all | solution.py:189
  95.5 2.2 gather_fusion.2
  97.9 1.8 fusion.26
  100.0 2.1 convolution_convert_fusion.3
  102.4 174.1 %all-gather.3.cloned.1.call-done = bf16[4096,2048]{1,0:T(8,128)(2,1)} async-done(((bf16[512,2048]{1,0:T(8,128)(2,1)}), bf16[4096,2048]{1,0:T(8,128)(2,1)}) %all-gather.3.cloned.1.call-update) | async-done | bytes 16777232 | tf_op jit(solution)/shard_map/all_gather | solution.py:10
  276.4 10.8 %reduce_sum.113 = bf16[512,2048]{1,0:T(8,128)(2,1)} reduce(bf16[8,512,2048]{2,1,0:T(8,128)(2,1)} %bitcast.163, bf16[]{:T(256)} %constant.89.clone.1), dimensions={0}, to_apply=%region_7.8 | reduce | flops 7340032 | bytes 18874370 | tf_op jit(solution)/shard_map/reduce_sum | solution.py:10
  287.2 3.5 fusion
  290.8 2.6 add_convert_fusion
  293.4 6.1 %convolution_convert_fusion.4 = bf16[512,2048]{1,0:T(8,128)(2,1)} fusion(bf16[512,2048]{1,0:T(8,128)(2,1)S(1)} %copy-done, bf16[512,2048]{1,0:T(8,128)(2,1)} %add_convert_fusion, bf16[2048,512]{1,0:T(8,128)(2,1)} %param.40, f32[512]{0:T(512)S(1)} %copy-done.12), kind=kOutput, calls=%fused_computation.14 | convolution fusion | flops 2151153664 | bytes 8390656 | tf_op jit(solution)/shard_map/dot_general | solution.py:217
  299.5 0.6 copy-done.9
  300.3 0.8 gather_fusion.3
  301.2 0.8 gather_fusion.4
  302.7 1.2 copy.80
  304.0 7.4 %all-to-all-start.3 = ((bf16[64,32,256]{2,1,0:T(8,128)(2,1)}), bf16[64,32,256]{2,1,0:T(8,128)(2,1)S(1)}, u32[]{:S(2)}, u32[]{:S(2)}) async-start(bf16[64,32,256]{2,1,0:T(8,128)(2,1)} %bitcast.48), calls=%async_computation.4 | async-start | bytes 2097152 | tf_op jit(solution)/shard_map/all_to_all | solution.py:148
  311.4 0.8 dynamic_slice.16
  312.1 0.8 dynamic_slice.18
  312.9 0.8 dynamic_slice.19
  313.7 12.1 %all-to-all-done.3 = bf16[64,32,256]{2,1,0:T(8,128)(2,1)S(1)} async-done(((bf16[64,32,256]{2,1,0:T(8,128)(2,1)}), bf16[64,32,256]{2,1,0:T(8,128)(2,1)S(1)}, u32[]{:S(2)}, u32[]{:S(2)}) %all-to-all-start.3) | async-done | bytes 1048608 | tf_op jit(solution)/shard_map/all_to_all | solution.py:148
  325.8 0.6 gather_fusion.5
  326.4 13.9 %reduce-scatter.2.cloned.1.call-done = bf16[512,256]{1,0:T(8,128)(2,1)} async-done(((bf16[512,2048]{1,0:T(8,128)(2,1)}), bf16[512,256]{1,0:T(8,128)(2,1)}) %reduce-scatter.2.cloned.1.call-update) | async-done | bytes 262160 | tf_op jit(solution)/shard_map/reduce_scatter | solution.py:216
  340.3 1.3 fusion.48
  341.5 0.6 broadcast_in_dim.71
  342.2 4.6 %all-to-all-start.2 = ((f32[8,2,512]{2,1,0:T(2,128)}), f32[8,2,512]{2,1,0:T(2,128)S(1)}, u32[]{:S(2)}, u32[]{:S(2)}) async-start(f32[8,2,512]{2,1,0:T(2,128)} %broadcast_in_dim.71), calls=%async_computation.3 | async-start | bytes 65536 | tf_op jit(solution)/shard_map/all_to_all | solution.py:228
  346.8 0.7 fusion.90
  347.4 7.4 %all-to-all-done.2 = f32[8,2,512]{2,1,0:T(2,128)S(1)} async-done(((f32[8,2,512]{2,1,0:T(2,128)}), f32[8,2,512]{2,1,0:T(2,128)S(1)}, u32[]{:S(2)}, u32[]{:S(2)}) %all-to-all-start.2) | async-done | bytes 32800 | tf_op jit(solution)/shard_map/all_to_all | solution.py:228
  354.8 1.9 add_convert_fusion.1
  (85 shorter events, 6.7 us)
Async XLA Ops:
  7.2 286.2 %copy-start = (bf16[512,2048]{1,0:T(8,128)(2,1)S(1)}, bf16[512,2048]{1,0:T(8,128)(2,1)}, u32[]{:S(2)}) copy-start(bf16[512,2048]{1,0:T(8,128)(2,1)} %param.42) | copy-start | bytes 6291460
  14.3 7.8 %copy-start.7 = (s32[256]{0:T(256)S(1)}, s32[256]{0:T(256)}, u32[]{:S(2)}) copy-start(s32[256]{0:T(256)} %param.25) | copy-start | bytes 3076
  14.3 9.0 %copy-start.10 = (s32[8]{0:T(128)S(1)}, s32[8]{0:T(128)}, u32[]{:S(2)}) copy-start(s32[8]{0:T(128)} %param.26) | copy-start | bytes 100
  14.3 9.0 %copy-start.8 = (s32[8,64]{1,0:T(8,128)S(1)}, s32[8,64]{1,0:T(8,128)}, u32[]{:S(2)}) copy-start(s32[8,64]{1,0:T(8,128)} %param.24) | copy-start | bytes 6148
  14.3 33.8 %all-to-all-start = ((bf16[64,64,256]{2,1,0:T(8,128)(2,1)}), bf16[64,64,256]{2,1,0:T(8,128)(2,1)}, u32[]{:S(2)}, u32[]{:S(2)}) async-start(bf16[64,64,256]{2,1,0:T(8,128)(2,1)} %bitcast.166), calls=%async_computation | async-start | bytes 4194304 | tf_op jit(solution)/shard_map/all_to_all | solution.py:145
  52.8 1.6 copy-start.11
  58.9 36.6 %all-to-all-start.1 = ((bf16[64,66,256]{2,1,0:T(8,128)(2,1)}), bf16[64,66,256]{2,1,0:T(8,128)(2,1)}, u32[]{:S(2)}, u32[]{:S(2)}) async-start(bf16[64,66,256]{2,1,0:T(8,128)(2,1)} %pad_maximum_fusion), calls=%async_computation.1 | async-start | bytes 4718592 | tf_op jit(solution)/shard_map/all_to_all | solution.py:189
  66.6 209.8 %all-gather.3.cloned.1.call-start = ((), (), s32[]{:S(2)}) async-start(), calls=%async_computation.6 | async-start | bytes 18874368 | tf_op jit(solution)/shard_map/all_gather | solution.py:10
  69.0 3.4 copy-start.13
  97.9 2.1 copy-start.3
  102.1 238.2 %reduce-scatter.2.cloned.1.call-start = ((), (), s32[]{:S(2)}) async-start(), calls=%async_computation.5 | async-start | bytes 2359296 | tf_op jit(solution)/shard_map/reduce_scatter | solution.py:216
  276.4 10.8 %copy-start.4 = (f32[2048]{0:T(1024)S(1)}, f32[2048]{0:T(1024)}, u32[]{:S(2)}) copy-start(f32[2048]{0:T(1024)} %param.37) | copy-start | bytes 24580
  287.2 3.5 copy-start.1
  287.2 3.5 copy-start.2
  287.2 3.5 copy-start.5
  287.2 3.5 copy-start.6
  290.8 2.6 copy-start.12
  299.5 0.7 copy-start.9
  299.5 2.6 copy-start.14
  304.0 21.9 %all-to-all-start.3 = ((bf16[64,32,256]{2,1,0:T(8,128)(2,1)}), bf16[64,32,256]{2,1,0:T(8,128)(2,1)S(1)}, u32[]{:S(2)}, u32[]{:S(2)}) async-start(bf16[64,32,256]{2,1,0:T(8,128)(2,1)} %bitcast.48), calls=%async_computation.4 | async-start | bytes 2097152 | tf_op jit(solution)/shard_map/all_to_all | solution.py:148
  342.2 12.6 %all-to-all-start.2 = ((f32[8,2,512]{2,1,0:T(2,128)}), f32[8,2,512]{2,1,0:T(2,128)S(1)}, u32[]{:S(2)}, u32[]{:S(2)}) async-start(f32[8,2,512]{2,1,0:T(2,128)} %broadcast_in_dim.71), calls=%async_computation.3 | async-start | bytes 65536 | tf_op jit(solution)/shard_map/all_to_all | solution.py:228
Sparse Core Ops, SparseCore 0:
  102.2 174.1 all-gather.2
  299.6 40.6 reduce-scatter.1
